TPU v7x, 32 devices: a whole 2x2x4 slice. The times are simulated.
32 devices in a mesh: ctx: 8 (over y, x, core), dp: 4 (over z).
Axes of the slice: x: 2, y: 2, z: 4, core: 2. Of those that a mesh axis runs over, the one named last changes fastest.
Arguments:
- tokens: bfloat16 [4, 1024, 4096], P('dp', 'ctx'), may hold values from -64 to 64
- query_weight: bfloat16 [4096, 4096], P('dp', 'ctx'), may hold values from -0.09375 to 0.09375
- keyval_matrix: bfloat16 [4096, 1024], P('dp', 'ctx'), may hold values from -0.09375 to 0.09375
- grad_out: bfloat16 [4, 1024, 4096], P('dp', 'ctx'), may hold values from -6 to 6
- blocks: int32 [4, 8, 8], replicated, may hold values from 0 to 7, as said below
- counts: int32 [4, 8], replicated, may hold values from 4 to 8, as said below
Outputs:
- attended: bfloat16 [4, 1024, 4096], P('dp', 'ctx')
- grad_query_weight: float32 [4096, 4096], P('dp', 'ctx')
- grad_keyval_weight: float32 [4096, 1024], P('dp', 'ctx')
Inputs may be any that keep to these rules, and one draw needn't show every extreme that they name: For key head g and query block i, the first counts[g, i] entries of blocks[g, i] are distinct; they are the blocks i - 1, i, i + 1, 0 and 7 that exist, then random others. Entries from counts[g, i] on are block numbers that are not attended. counts[g, i] is the number of distinct blocks among i - 1, i, i + 1, 0 and 7 that exist, plus 1 to 3.
All inputs are finite; a program needn't handle non-finite values.
Results may differ from a plain program's by a relative error of at most 0.004.
The roundings to bfloat16 on the way count: a program that leaves them out, or rounds other values in their place, can miss the bound.
Values may be sent and summed in bfloat16 or wider, within the bound.
No kernel may reach another device: no remote copies, remote signals or barrier semaphores. Data moves between devices by JAX's collectives and lax.ppermute only.
A program may use at most 128 MiB of HBM per device.

v0:
```python
import jax
import jax.numpy as jnp
from jax import lax
from jax.sharding import PartitionSpec as P


def partner(block, axis, distance):
    count = lax.axis_size(axis)
    route = []
    for low in range(count):
        high = low | 1 << distance
        if high != low and high < count:
            route += [(low, high), (high, low)]
    return lax.ppermute(block, axis, route)


def attend_part(query_rows, key_rows, vals, dout, valid, scale):
    scores = (
        jnp.einsum("nqhd,nkcd->nhqkc", query_rows, key_rows, preferred_element_type=jnp.float32)
        * scale
    )
    scores = jnp.where(valid[:, None, None, :, None], scores, -jnp.inf)
    peak = jnp.max(scores, axis=(3, 4), keepdims=True)
    expo = jnp.exp(scores - peak)
    probs = expo / jnp.sum(expo, axis=(3, 4), keepdims=True)
    probs_b = probs.astype(jnp.bfloat16)
    out = jnp.einsum("nhqkc,nkcd->nqhd", probs_b, vals, preferred_element_type=jnp.float32).astype(
        jnp.bfloat16
    )
    delta = jnp.transpose(
        jnp.sum(dout.astype(jnp.float32) * out.astype(jnp.float32), axis=3), (0, 2, 1)
    )
    dprob = jnp.einsum("nqhd,nkcd->nhqkc", dout, vals, preferred_element_type=jnp.float32)
    dscore = (probs * (dprob - delta[:, :, :, None, None]) * scale).astype(jnp.bfloat16)
    dquery = jnp.einsum(
        "nhqkc,nkcd->nqhd", dscore, key_rows, preferred_element_type=jnp.float32
    ).astype(jnp.bfloat16)
    dkeys = jnp.einsum("nhqkc,nqhd->nkcd", dscore, query_rows, preferred_element_type=jnp.float32)
    dvals = jnp.einsum("nhqkc,nqhd->nkcd", probs_b, dout, preferred_element_type=jnp.float32)
    return (out, dquery, dkeys, dvals)


def attention(q_heads, keyval_rows, dout_heads, blk, cnt):
    length = q_heads.shape[0]
    head_size = keyval_rows.shape[1] // 2
    heads = q_heads.shape[1] // head_size
    nblocks, kslots = blk.shape
    block = length // nblocks
    scale = head_size ** (-0.5)
    step = 4
    groups = nblocks // step
    key_rows = keyval_rows[:, :head_size].reshape(nblocks, block, head_size)
    vals = keyval_rows[:, head_size:].reshape(nblocks, block, head_size)
    valid = lax.broadcasted_iota(jnp.int32, (nblocks, kslots), 1) < cnt[:, None]
    query_rows = q_heads.reshape(groups, step, block, heads, head_size)
    dout = dout_heads.reshape(groups, step, block, heads, head_size)

    def one_step(args):
        q_part, d_part, b_part, v_part = args
        return attend_part(q_part, key_rows[b_part], vals[b_part], d_part, v_part, scale)

    out, dquery, dkeys, dvals = lax.map(
        one_step,
        (query_rows, dout, blk.reshape(groups, step, kslots), valid.reshape(groups, step, kslots)),
    )
    dkeys = dkeys.reshape(nblocks, kslots, block, head_size)
    dvals = dvals.reshape(nblocks, kslots, block, head_size)
    onehot = (
        (blk[None, :, :] == lax.broadcasted_iota(jnp.int32, (nblocks, 1, 1), 0)) & valid[None]
    ).astype(jnp.float32)
    key_grad = jnp.einsum("bnk,nkcd->bcd", onehot, dkeys, precision=lax.Precision.HIGHEST)
    val_grad = jnp.einsum("bnk,nkcd->bcd", onehot, dvals, precision=lax.Precision.HIGHEST)
    keyval_grad = jnp.concatenate(
        [key_grad.reshape(length, head_size), val_grad.reshape(length, head_size)], axis=1
    )
    return (
        out.reshape(length, heads * head_size),
        dquery.reshape(length, heads * head_size),
        keyval_grad,
    )


def shards(tokens, query_weight, keyval_matrix, grad_out, blocks, counts):
    local_rows = tokens[0]
    group_size = lax.axis_size("ctx") // blocks.shape[0]
    group_bits = group_size.bit_length() - 1
    device = lax.axis_index("ctx")
    query_cols = query_weight.shape[1]
    query_full, keyval_part = (
        lax.all_gather(query_weight, "dp", axis=0, tiled=True),
        lax.all_gather(keyval_matrix, "dp", axis=0, tiled=True),
    )
    all_rows = lax.all_gather(local_rows, "ctx", axis=0, tiled=True)
    keyval_cols = keyval_part
    for bit in range(group_bits):
        other = partner(keyval_cols, "ctx", bit)
        upper = device >> bit & 1 == 1
        keyval_cols = jnp.where(
            upper,
            jnp.concatenate([other, keyval_cols], axis=1),
            jnp.concatenate([keyval_cols, other], axis=1),
        )
    projected = jnp.dot(
        all_rows,
        jnp.concatenate([query_full, keyval_cols], axis=1),
        preferred_element_type=jnp.float32,
    ).astype(jnp.bfloat16)
    q_heads = projected[:, :query_cols]
    keyval_rows = projected[:, query_cols:]
    dout_heads = lax.all_to_all(grad_out[0], "ctx", split_axis=1, concat_axis=0, tiled=True)
    group_index = device // group_size
    blk = lax.dynamic_index_in_dim(blocks, group_index, 0, keepdims=False)
    cnt = lax.dynamic_index_in_dim(counts, group_index, 0, keepdims=False)
    out_heads, dquery, keyval_grad = attention(q_heads, keyval_rows, dout_heads, blk, cnt)
    attended = lax.all_to_all(out_heads, "ctx", split_axis=0, concat_axis=1, tiled=True)
    summed = keyval_grad
    for bit in range(group_bits):
        summed = summed + partner(summed, "ctx", bit)
    width = summed.shape[1] // group_size
    own_grad = lax.dynamic_slice_in_dim(summed, device % group_size * width, width, 1)
    own_grad = own_grad.astype(jnp.bfloat16)
    contract = (((0,), (0,)), ((), ()))
    grad_query = lax.dot_general(all_rows, dquery, contract, preferred_element_type=jnp.float32)
    grad_keyval = lax.dot_general(all_rows, own_grad, contract, preferred_element_type=jnp.float32)
    grad_query, grad_keyval = (
        lax.psum_scatter(grad_query, "dp", scatter_dimension=0, tiled=True),
        lax.psum_scatter(grad_keyval, "dp", scatter_dimension=0, tiled=True),
    )
    return (attended[None], grad_query, grad_keyval)


def solution(mesh):
    in_specs = (
        P("dp", "ctx", None),
        P("dp", "ctx"),
        P("dp", "ctx"),
        P("dp", "ctx", None),
        P(),
        P(),
    )
    out_specs = (P("dp", "ctx", None), P("dp", "ctx"), P("dp", "ctx"))
    return jax.shard_map(shards, mesh=mesh, in_specs=in_specs, out_specs=out_specs, check_vma=False)
```

profile of v0, /device:TPU:0, one launch (start us, length us, event | category | flops | bytes accessed | tf_op | source)
XLA Modules:
  0.0 476.1 jit_solution(6639766574015722503)
XLA Ops:
  9.4 30.8 %all-gather.7.cloned.1.call-done = bf16[4096,128]{1,0:T(8,128)(2,1)} async-done(((bf16[1024,128]{1,0:T(8,128)(2,1)}), bf16[4096,128]{1,0:T(8,128)(2,1)}) %all-gather.7.cloned.1.call-update) | async-done | bytes 1048592 | tf_op jit(solution)/shard_map/all_gather | solution.py:91
  42.5 4.2 all-to-all-start
  49.0 3.1 maximum_select_fusion
  52.1 70.0 %all-gather.5.cloned.1.call-done = bf16[4096,512]{1,0:T(8,128)(2,1)} async-done(((bf16[1024,512]{1,0:T(8,128)(2,1)}), bf16[4096,512]{1,0:T(8,128)(2,1)}) %all-gather.5.cloned.1.call-update) | async-done | bytes 4194320 | tf_op jit(solution)/shard_map/all_gather | solution.py:90
  122.1 54.8 %all-gather.9.cloned.1.call-done = bf16[1,1024,4096]{2,1,0:T(8,128)(2,1)} async-done(((bf16[1,128,4096]{2,1,0:T(8,128)(2,1)}), bf16[1,1024,4096]{2,1,0:T(8,128)(2,1)}) %all-gather.9.cloned.1.call-update) | async-done | bytes 8388624 | tf_op jit(solution)/shard_map/all_gather | solution.py:93
  177.0 10.4 %fusion.56 = bf16[1024,768]{0,1:T(8,128)(2,1)S(1)} fusion(bf16[1,1024,4096]{2,1,0:T(8,128)(2,1)} %all-gather.9.cloned.1.call-done, bf16[4096,256]{1,0:T(8,128)(2,1)S(1)} %maximum_select_fusion, bf16[4096,512]{1,0:T(8,128)(2,1)} %all-gather.5.cloned.1.call-done), kind=kOutput, calls=%fused_computation.57 | convolution fusion | flops 6455820288 | bytes 16252928 | tf_op jit(solution)/shard_map/dot_general | solution.py:103
  189.4 65.5 %while.16 = (s32[]{:T(128)}, bf16[2,4,128,4,128]{2,4,3,1,0:T(8,128)(2,1)}, bf16[2,4,128,4,128]{4,3,2,1,0:T(4,128)(2,1)}, f32[2,4,8,128,128]{4,3,2,1,0:T(8,128)},...) while((s32[]{:T(128)}, ...), condition=%wide.region_4.5_spmd, body=%wide.region_0.4_spmd.sunk | while | flops 3275222016 | bytes 218726320 | solution.py:62
  195.2 3.4 copy-done.6
  198.6 3.2 bitcast_dynamic-update-slice_fusion.8
  204.6 6.5 %bitcast_dynamic-update-slice_fusion.6 = (bf16[2,4,128,4,128]{2,4,3,1,0:T(8,128)(2,1)}, bf16[4,128,4,128]{3,1,2,0:T(8,128)(2,1)S(1)}) fusion(bf16[2,4,128,4,128]{2,4,3,1,0:T(8,128)(2,1)} %get-tuple-element.241, s32[]{:T(128)} %get-tuple-element.240, bf16[4,8,128,128,1]{3,2,4,1,0:T(8,128)(2,1)S(1)} %bitcast.231, f32[4,4,128]{2,1,0:T(4,128)S(1)} %fusion.119, ...), kind=kOutput, calls=%fused_computation.26.clone.1 | convolution fusion | flops 547618816 | bytes 10502688 | tf_op jit(solution)/shard_map/while/body/eval_jaxpr/nhqkc,nkcd->nqhd/dot_general | solution.py:27
  212.3 4.3 fusion.120
  227.9 3.4 copy-done.6
  231.2 3.2 bitcast_dynamic-update-slice_fusion.8
  237.2 6.5 %bitcast_dynamic-update-slice_fusion.6 = (bf16[2,4,128,4,128]{2,4,3,1,0:T(8,128)(2,1)}, bf16[4,128,4,128]{3,1,2,0:T(8,128)(2,1)S(1)}) fusion(bf16[2,4,128,4,128]{2,4,3,1,0:T(8,128)(2,1)} %get-tuple-element.241, s32[]{:T(128)} %get-tuple-element.240, bf16[4,8,128,128,1]{3,2,4,1,0:T(8,128)(2,1)S(1)} %bitcast.231, f32[4,4,128]{2,1,0:T(4,128)S(1)} %fusion.119, ...), kind=kOutput, calls=%fused_computation.26.clone.1 | convolution fusion | flops 547618816 | bytes 10502688 | tf_op jit(solution)/shard_map/while/body/eval_jaxpr/nhqkc,nkcd->nqhd/dot_general | solution.py:27
  245.0 4.3 fusion.120
  254.9 7.2 %fusion.61 = f32[8,128,128]{2,0,1:T(8,128)S(1)} fusion(f32[8,8,128,128]{3,2,1,0:T(8,128)} %bitcast.237, s32[8,8]{0,1:T(8,128)S(1)} %copy-done.13, pred[8,8]{0,1:T(8,128)(4,1)S(1)} %copy-done.14), kind=kOutput, calls=%fused_computation.61 | convolution fusion | flops 100664320 | bytes 4718912 | tf_op jit(solution)/shard_map/bnk,nkcd->bcd/dot_general | solution.py:71
  262.3 5.0 %fusion.64 = f32[8,128,128]{2,0,1:T(8,128)S(1)} fusion(f32[8,8,128,128]{3,2,1,0:T(8,128)S(1)} %bitcast.238, s32[8,8]{0,1:T(8,128)S(1)} %copy-done.13, pred[8,8]{0,1:T(8,128)(4,1)S(1)} %copy-done.14), kind=kOutput, calls=%fused_computation.62 | convolution fusion | flops 100664320 | bytes 4718912 | tf_op jit(solution)/shard_map/bnk,nkcd->bcd/dot_general | solution.py:72
  267.8 2.5 collective-permute-done.1
  270.3 6.2 %fusion.44 = f32[4096,128]{0,1:T(8,128)} fusion(bf16[1,1024,4096]{2,1,0:T(8,128)(2,1)} %all-gather.9.cloned.1.call-done, s32[]{:T(128)S(6)} %select_n.51, f32[1024,128]{1,0:T(8,128)S(1)} %bitcast.234, f32[1024,128]{1,0:T(8,128)S(1)} %bitcast.236, f32[1024,256]{1,0:T(8,128)} %collective-permute-done.1), kind=kOutput, calls=%fused_computation.50 | convolution fusion | flops 1074135040 | bytes 12058628 | tf_op jit(solution)/shard_map/dot_general | solution.py:124
  276.6 10.4 %fusion.38 = f32[4096,512]{0,1:T(8,128)} fusion(bf16[1,1024,4096]{2,1,0:T(8,128)(2,1)} %all-gather.9.cloned.1.call-done, bf16[128,8,4,128]{3,2,1,0:T(4,128)(2,1)S(1)} %bitcast.240), kind=kOutput, calls=%fused_computation.46 | convolution fusion | flops 4294967296 | bytes 17825792 | tf_op jit(solution)/shard_map/dot_general | solution.py:123
  288.7 17.9 %all_to_all.32 = bf16[8,128,512]{2,1,0:T(8,128)(2,1)S(1)} all-to-all(bf16[8,128,512]{2,1,0:T(8,128)(2,1)S(1)} %copy.112), channel_id=1, replica_groups=mesh['ctx'=8,'dp'=4] {'ctx'}, dimensions={0} | all-to-all | bytes 2097152 | tf_op jit(solution)/shard_map/all_to_all | solution.py:115
  308.6 11.9 %reduce-scatter.5.cloned.1.call-done = f32[1024,128]{0,1:T(8,128)} async-done(((f32[4096,128]{0,1:T(8,128)}), f32[1024,128]{0,1:T(8,128)}) %reduce-scatter.5.cloned.1.call-update) | async-done | bytes 524304 | tf_op jit(solution)/shard_map/reduce_scatter | solution.py:127
  322.6 144.1 %reduce-scatter.3.cloned.1.call-done = f32[1024,512]{0,1:T(8,128)} async-done(((f32[4096,512]{0,1:T(8,128)}), f32[1024,512]{0,1:T(8,128)}) %reduce-scatter.3.cloned.1.call-update) | async-done | bytes 2097168 | tf_op jit(solution)/shard_map/reduce_scatter | solution.py:126
  466.7 2.9 copy.82
  (112 shorter events, 45.2 us)
Async XLA Ops:
  7.2 40.5 %copy-start = (s32[4,8,8]{2,1,0:T(8,128)S(1)}, s32[4,8,8]{2,1,0:T(8,128)}, u32[]{:S(2)}) copy-start(s32[4,8,8]{2,1,0:T(8,128)} %param.12) | copy-start | bytes 3076
  7.2 33.1 %all-gather.7.cloned.1.call-start = ((), (), s32[]{:S(2)}) async-start(), calls=%async_computation.5 | async-start | bytes 1310720 | tf_op jit(solution)/shard_map/all_gather | solution.py:91
  7.9 114.2 %all-gather.5.cloned.1.call-start = ((), (), s32[]{:S(2)}) async-start(), calls=%async_computation.4 | async-start | bytes 5242880 | tf_op jit(solution)/shard_map/all_gather | solution.py:90
  8.7 168.3 %all-gather.9.cloned.1.call-start = ((), (), s32[]{:S(2)}) async-start(), calls=%async_computation.8 | async-start | bytes 9437184 | tf_op jit(solution)/shard_map/all_gather | solution.py:93
  40.2 8.8 %collective-permute-start = (bf16[4096,128]{1,0:T(8,128)(2,1)}, bf16[4096,128]{1,0:T(8,128)(2,1)}, u32[]{:S(2)}, u32[]{:S(2)}) collective-permute-start(bf16[4096,128]{1,0:T(8,128)(2,1)} %all-gather.7.cloned.1.call-done), channel_id=1, source_target_pairs={{0,4},{4,0},{8,12},{12,8},{16,20},{20,16},{24,28},{28,24},{1,5},{5... | collective-permute-start | bytes 3145736 | tf_op jit(solution)/shard_map/ppermute | solution.py:14
  42.5 146.9 %all-to-all-start = ((bf16[128,8,512]{0,2,1:T(8,128)(2,1)}), bf16[128,8,512]{0,2,1:T(8,128)(2,1)}, u32[]{:S(2)}, u32[]{:S(2)}) async-start(bf16[128,8,512]{0,2,1:T(8,128)(2,1)} %bitcast.39), calls=%async_computation | async-start | bytes 2097152 | tf_op jit(solution)/shard_map/all_to_all | solution.py:110
  46.8 273.8 %reduce-scatter.5.cloned.1.call-start = ((), (), s32[]{:S(2)}) async-start(), calls=%async_computation.7 | async-start | bytes 2621440 | tf_op jit(solution)/shard_map/reduce_scatter | solution.py:127
  189.4 65.5 %copy-start.13 = (s32[8,8]{0,1:T(8,128)S(1)}, s32[8,8]{0,1:T(8,128)}, u32[]{:S(2)}) copy-start(s32[8,8]{0,1:T(8,128)} %copy.76) | copy-start | bytes 772
  189.4 65.5 %copy-start.14 = (pred[8,8]{0,1:T(8,128)(4,1)S(1)}, pred[8,8]{0,1:T(8,128)(4,1)}, u32[]{:S(2)}) copy-start(pred[8,8]{0,1:T(8,128)(4,1)} %iota_compare_fusion.1) | copy-start | bytes 196
  193.4 8.4 %copy-start.2 = (f32[4,8,128,128,4]{3,2,4,1,0:T(8,128)}, f32[4,8,128,128,4]{3,2,4,1,0:T(8,128)S(1)}, u32[]{:S(2)}) copy-start(f32[4,8,128,128,4]{3,2,4,1,0:T(8,128)S(1)} %get-tuple-element.224) | copy-start | bytes 25165828 | tf_op jit(solution)/shard_map/while
  193.4 5.2 %copy-start.6 = (f32[2,4,8,128,128]{4,3,2,1,0:T(8,128)S(1)}, f32[2,4,8,128,128]{4,3,2,1,0:T(8,128)}, u32[]{:S(2)}) copy-start(f32[2,4,8,128,128]{4,3,2,1,0:T(8,128)} %get-tuple-element.244) | copy-start | bytes 12582916 | tf_op jit(solution)/shard_map/while
  204.5 7.8 %copy-start.3 = (f32[4,8,128,128,4]{3,2,4,1,0:T(8,128)S(1)}, f32[4,8,128,128,4]{3,2,4,1,0:T(8,128)}, u32[]{:S(2)}) copy-start(f32[4,8,128,128,4]{3,2,4,1,0:T(8,128)} %copy-done.2) | copy-start | bytes 25165828 | tf_op jit(solution)/shard_map/while
  212.3 4.4 copy-start.4
  216.7 4.4 copy-start.9
  226.0 8.4 %copy-start.2 = (f32[4,8,128,128,4]{3,2,4,1,0:T(8,128)}, f32[4,8,128,128,4]{3,2,4,1,0:T(8,128)S(1)}, u32[]{:S(2)}) copy-start(f32[4,8,128,128,4]{3,2,4,1,0:T(8,128)S(1)} %get-tuple-element.224) | copy-start | bytes 25165828 | tf_op jit(solution)/shard_map/while
  226.0 5.2 %copy-start.6 = (f32[2,4,8,128,128]{4,3,2,1,0:T(8,128)S(1)}, f32[2,4,8,128,128]{4,3,2,1,0:T(8,128)}, u32[]{:S(2)}) copy-start(f32[2,4,8,128,128]{4,3,2,1,0:T(8,128)} %get-tuple-element.244) | copy-start | bytes 12582916 | tf_op jit(solution)/shard_map/while
  237.2 7.8 %copy-start.3 = (f32[4,8,128,128,4]{3,2,4,1,0:T(8,128)S(1)}, f32[4,8,128,128,4]{3,2,4,1,0:T(8,128)}, u32[]{:S(2)}) copy-start(f32[4,8,128,128,4]{3,2,4,1,0:T(8,128)} %copy-done.2) | copy-start | bytes 25165828 | tf_op jit(solution)/shard_map/while
  245.0 4.4 copy-start.4
  249.3 4.4 copy-start.9
  254.9 7.4 %copy-start.8 = (f32[2,4,8,128,128]{4,3,2,1,0:T(8,128)S(1)}, f32[2,4,8,128,128]{4,3,2,1,0:T(8,128)}, u32[]{:S(2)}) copy-start(f32[2,4,8,128,128]{4,3,2,1,0:T(8,128)} %get-tuple-element.66) | copy-start | bytes 12582916
  267.5 2.9 collective-permute-start.1
  267.8 8.8 %copy-start.11 = (bf16[2,4,128,4,128]{4,3,2,1,0:T(4,128)(2,1)S(1)}, bf16[2,4,128,4,128]{4,3,2,1,0:T(4,128)(2,1)}, u32[]{:S(2)}) copy-start(bf16[2,4,128,4,128]{4,3,2,1,0:T(4,128)(2,1)} %get-tuple-element.64) | copy-start | bytes 3145732
  276.5 190.2 %reduce-scatter.3.cloned.1.call-start = ((), (), s32[]{:S(2)}) async-start(), calls=%async_computation.6 | async-start | bytes 10485760 | tf_op jit(solution)/shard_map/reduce_scatter | solution.py:126
  288.2 181.4 %copy-start.1 = (s32[4,8,8]{2,1,0:T(8,128)S(1)}, s32[4,8,8]{2,1,0:T(8,128)}, u32[]{:S(2)}) copy-start(s32[4,8,8]{2,1,0:T(8,128)} %param.12) | copy-start | bytes 3076
  (7 other events, 11.1 us)
Sparse Core Ops, SparseCore 0:
  9.6 30.6 all-gather.6
  41.8 80.2 all-gather.4
  124.0 52.9 all-gather.8
  276.6 43.8 reduce-scatter.4
  322.9 143.8 reduce-scatter.2
where the time goes:
time: 477 us; the launch traced here: 476 us
  waiting for transfers between devices  316 us (66%)
  matrix products  74 us (16%)
  local copies, waits for them, and re-layouts  38.6 us (8%)
  blocking collectives  17.9 us (4%)
  between operations  14 us (3%)
  other arithmetic  9.91 us (2%)
    reduce_scatter x1, waiting for transfers between devices, shards(): lax.psum_scatter(grad_query, 'dp', scatter_dimension=0, tiled=True)  144 us
    all_gather x1, waiting for transfers between devices, shards(): lax.all_gather(query_weight, 'dp', axis=0, tiled=True)  70 us
    all_gather x1, waiting for transfers between devices, shards(): all_rows = lax.all_gather(local_rows, 'ctx', axis=0, tiled=True)  54.8 us
    all_gather x1, waiting for transfers between devices, shards(): lax.all_gather(keyval_matrix, 'dp', axis=0, tiled=True)  30.8 us
    all_to_all x1, blocking collectives, shards(): lax.all_to_all(out_heads, 'ctx', split_axis=0, concat_axis=1, tiled=True)  17.9 us
    while x32, local copies, waits for them, and re-layouts  16.6 us
    dot_general x2, matrix products, attend_part(): jnp.einsum('nhqkc,nkcd->nqhd', probs_b, vals, preferred_element_type=jnp....  13.1 us
    reduce_scatter x1, waiting for transfers between devices, shards(): lax.psum_scatter(grad_keyval, 'dp', scatter_dimension=0, tiled=True)  11.9 us
  transfers between devices with their start and end apart: 8, of which 6 were waited for; matrix products, arithmetic and copies ran while one was open for 7% of the time, Pallas kernels for 0%

commit v1 on v0

--- a/solution.py
+++ b/solution.py
@@ -86,10 +86,11 @@
     group_bits = group_size.bit_length() - 1
     device = lax.axis_index("ctx")
     query_cols = query_weight.shape[1]
-    query_full, keyval_part = (
-        lax.all_gather(query_weight, "dp", axis=0, tiled=True),
-        lax.all_gather(keyval_matrix, "dp", axis=0, tiled=True),
+    weights_full = lax.all_gather(
+        jnp.concatenate([query_weight, keyval_matrix], axis=1), "dp", axis=0, tiled=True
     )
+    query_full = weights_full[:, :query_cols]
+    keyval_part = weights_full[:, query_cols:]
     all_rows = lax.all_gather(local_rows, "ctx", axis=0, tiled=True)
     keyval_cols = keyval_part
     for bit in range(group_bits):
@@ -122,10 +123,11 @@
     contract = (((0,), (0,)), ((), ()))
     grad_query = lax.dot_general(all_rows, dquery, contract, preferred_element_type=jnp.float32)
     grad_keyval = lax.dot_general(all_rows, own_grad, contract, preferred_element_type=jnp.float32)
-    grad_query, grad_keyval = (
-        lax.psum_scatter(grad_query, "dp", scatter_dimension=0, tiled=True),
-        lax.psum_scatter(grad_keyval, "dp", scatter_dimension=0, tiled=True),
+    grads = lax.psum_scatter(
+        jnp.concatenate([grad_query, grad_keyval], axis=1), "dp", scatter_dimension=0, tiled=True
     )
+    grad_query = grads[:, :query_cols]
+    grad_keyval = grads[:, query_cols:]
     return (attended[None], grad_query, grad_keyval)
 
 

time: 477 us -> 478 us (level)
  waiting for transfers between devices: 316 us -> 304 us
  other arithmetic: 9.91 us -> 20.1 us
    concatenate x0 -> x2, other arithmetic: none -> 11.2 us  [the longest x1 8.64 us: shards(): jnp.concatenate([grad_query, grad_keyval], axis=1)]
    all_gather x1, waiting for transfers between devices: 54.8 us -> 46.3 us  [shards(): all_rows = lax.all_gather(local_rows, 'ctx', axis=0, tiled=True)]
    slice x0 -> x6, local copies, waits for them, and re-layouts: none -> 7.49 us  [the longest x1 4.61 us: shards(): query_full = weights_full[:, :query_cols]]
    reduce_scatter x2 -> x1, waiting for transfers between devices: 156 us -> 157 us  [shards(): lax.psum_scatter(jnp.concatenate([grad_query, grad_keyval], axis=1), 'dp'...]
    all_gather x2 -> x1, waiting for transfers between devices: 101 us -> 100 us  [shards(): lax.all_gather(jnp.concatenate([query_weight, keyval_matrix], axis=1), 'd...]
  transfers between devices with their start and end apart: 8 -> 6, of which waited for: 6 -> 3; matrix products, arithmetic and copies ran while one was open for 7% -> 8% of each run, Pallas kernels for 0% -> 0%
where the time goes in v1:
time: 478 us; the launch traced here: 477 us
  waiting for transfers between devices  304 us (64%)
  matrix products  72.5 us (15%)
  local copies, waits for them, and re-layouts  43 us (9%)
  other arithmetic  20.1 us (4%)
  blocking collectives  17.9 us (4%)
  between operations  14 us (3%)
    reduce_scatter x1, waiting for transfers between devices, shards(): lax.psum_scatter(jnp.concatenate([grad_query, grad_keyval], axis=1), 'dp'...  157 us
    all_gather x1, waiting for transfers between devices, shards(): lax.all_gather(jnp.concatenate([query_weight, keyval_matrix], axis=1), 'd...  100 us
    all_gather x1, waiting for transfers between devices, shards(): all_rows = lax.all_gather(local_rows, 'ctx', axis=0, tiled=True)  46.3 us
    all_to_all x1, blocking collectives, shards(): lax.all_to_all(out_heads, 'ctx', split_axis=0, concat_axis=1, tiled=True)  17.9 us
    while x32, local copies, waits for them, and re-layouts  16.5 us
    dot_general x2, matrix products, attend_part(): jnp.einsum('nhqkc,nkcd->nqhd', probs_b, vals, preferred_element_type=jnp....  13.1 us
    dot_general x1, matrix products, shards(): jnp.dot(all_rows, jnp.concatenate([query_full, keyval_cols], axis=1), pre...  10.4 us
    dot_general x1, matrix products, shards(): lax.dot_general(all_rows, dquery, contract, preferred_element_type=jnp.fl...  10.2 us
  transfers between devices with their start and end apart: 6, of which 3 were waited for; matrix products, arithmetic and copies ran while one was open for 8% of the time, Pallas kernels for 0%

profile of v1, /device:TPU:0, one launch (start us, length us, event | category | flops | bytes accessed | tf_op | source)
XLA Modules:
  0.0 476.8 jit_solution(18149583840988707000)
XLA Ops:
  7.2 2.6 pad_maximum_fusion.1
  10.6 100.4 %all-gather.4.cloned.1.call-done = bf16[4096,640]{1,0:T(8,128)(2,1)} async-done(((bf16[1024,640]{1,0:T(8,128)(2,1)}), bf16[4096,640]{1,0:T(8,128)(2,1)}) %all-gather.4.cloned.1.call-update) | async-done | bytes 5242896 | tf_op jit(solution)/shard_map/all_gather | solution.py:89
  113.6 4.2 all-to-all-start
  120.1 4.6 slice.35
  124.7 2.1 maximum_select_fusion
  126.9 46.3 %all-gather.6.cloned.1.call-done = bf16[1,1024,4096]{2,1,0:T(8,128)(2,1)} async-done(((bf16[1,128,4096]{2,1,0:T(8,128)(2,1)}), bf16[1,1024,4096]{2,1,0:T(8,128)(2,1)}) %all-gather.6.cloned.1.call-update) | async-done | bytes 8388624 | tf_op jit(solution)/shard_map/all_gather | solution.py:94
  173.1 10.4 %fusion.56 = bf16[1024,768]{0,1:T(8,128)(2,1)S(1)} fusion(bf16[1,1024,4096]{2,1,0:T(8,128)(2,1)} %all-gather.6.cloned.1.call-done, bf16[4096,256]{1,0:T(8,128)(2,1)S(1)} %maximum_select_fusion, bf16[4096,512]{1,0:T(8,128)(2,1)} %slice.35), kind=kOutput, calls=%fused_computation.58 | convolution fusion | flops 6455820288 | bytes 16252928 | tf_op jit(solution)/shard_map/dot_general | solution.py:104
  185.6 65.5 %while.16 = (s32[]{:T(128)}, bf16[2,4,128,4,128]{2,4,3,1,0:T(8,128)(2,1)}, bf16[2,4,128,4,128]{4,3,2,1,0:T(4,128)(2,1)}, f32[2,4,8,128,128]{4,3,2,1,0:T(8,128)},...) while((s32[]{:T(128)}, ...), condition=%wide.region_4.5_spmd, body=%wide.region_0.4_spmd.sunk | while | flops 3275222016 | bytes 218726320 | solution.py:62
  191.4 3.4 copy-done.6
  194.8 3.2 bitcast_dynamic-update-slice_fusion.8
  200.7 6.5 %bitcast_dynamic-update-slice_fusion.6 = (bf16[2,4,128,4,128]{2,4,3,1,0:T(8,128)(2,1)}, bf16[4,128,4,128]{3,1,2,0:T(8,128)(2,1)S(1)}) fusion(bf16[2,4,128,4,128]{2,4,3,1,0:T(8,128)(2,1)} %get-tuple-element.241, s32[]{:T(128)} %get-tuple-element.240, bf16[4,8,128,128,1]{3,2,4,1,0:T(8,128)(2,1)S(1)} %bitcast.231, f32[4,4,128]{2,1,0:T(4,128)S(1)} %fusion.119, ...), kind=kOutput, calls=%fused_computation.26.clone.1 | convolution fusion | flops 547618816 | bytes 10502688 | tf_op jit(solution)/shard_map/while/body/eval_jaxpr/nhqkc,nkcd->nqhd/dot_general | solution.py:27
  208.5 4.3 fusion.120
  214.1 2.0 copy-done.5
  224.0 3.4 copy-done.6
  227.4 3.2 bitcast_dynamic-update-slice_fusion.8
  233.3 6.5 %bitcast_dynamic-update-slice_fusion.6 = (bf16[2,4,128,4,128]{2,4,3,1,0:T(8,128)(2,1)}, bf16[4,128,4,128]{3,1,2,0:T(8,128)(2,1)S(1)}) fusion(bf16[2,4,128,4,128]{2,4,3,1,0:T(8,128)(2,1)} %get-tuple-element.241, s32[]{:T(128)} %get-tuple-element.240, bf16[4,8,128,128,1]{3,2,4,1,0:T(8,128)(2,1)S(1)} %bitcast.231, f32[4,4,128]{2,1,0:T(4,128)S(1)} %fusion.119, ...), kind=kOutput, calls=%fused_computation.26.clone.1 | convolution fusion | flops 547618816 | bytes 10502688 | tf_op jit(solution)/shard_map/while/body/eval_jaxpr/nhqkc,nkcd->nqhd/dot_general | solution.py:27
  241.1 4.3 fusion.120
  251.1 7.2 %fusion.61 = f32[8,128,128]{2,0,1:T(8,128)S(1)} fusion(f32[8,8,128,128]{3,2,1,0:T(8,128)} %bitcast.237, s32[8,8]{0,1:T(8,128)S(1)} %copy-done.14, pred[8,8]{0,1:T(8,128)(4,1)S(1)} %copy-done.15), kind=kOutput, calls=%fused_computation.63 | convolution fusion | flops 100664320 | bytes 4718912 | tf_op jit(solution)/shard_map/bnk,nkcd->bcd/dot_general | solution.py:71
  258.4 5.0 %fusion.64 = f32[8,128,128]{2,0,1:T(8,128)S(1)} fusion(f32[8,8,128,128]{3,2,1,0:T(8,128)S(1)} %bitcast.238, s32[8,8]{0,1:T(8,128)S(1)} %copy-done.14, pred[8,8]{0,1:T(8,128)(4,1)S(1)} %copy-done.15), kind=kOutput, calls=%fused_computation.64 | convolution fusion | flops 100664320 | bytes 4718912 | tf_op jit(solution)/shard_map/bnk,nkcd->bcd/dot_general | solution.py:72
  263.9 10.2 %fusion.38 = f32[4096,512]{0,1:T(8,128)} fusion(bf16[1,1024,4096]{2,1,0:T(8,128)(2,1)} %all-gather.6.cloned.1.call-done, bf16[128,8,4,128]{3,2,1,0:T(4,128)(2,1)S(1)} %bitcast.240), kind=kOutput, calls=%fused_computation.47 | convolution fusion | flops 4294967296 | bytes 17825792 | tf_op jit(solution)/shard_map/dot_general | solution.py:124
  274.1 4.9 %fusion.44 = f32[4096,128]{0,1:T(8,128)S(1)} fusion(bf16[1,1024,4096]{2,1,0:T(8,128)(2,1)} %all-gather.6.cloned.1.call-done, s32[]{:T(128)S(6)} %select_n.51, f32[1024,128]{1,0:T(8,128)S(1)} %bitcast.234, f32[1024,128]{1,0:T(8,128)S(1)} %bitcast.236, f32[1024,256]{1,0:T(8,128)} %collective-permute-done.1), kind=kOutput, calls=%fused_computation.51 | convolution fusion | flops 1074135040 | bytes 12058628 | tf_op jit(solution)/shard_map/dot_general | solution.py:125
  279.0 8.6 %pad_maximum_fusion = f32[4096,640]{0,1:T(8,128)} fusion(f32[4096,128]{0,1:T(8,128)S(1)} %fusion.44, f32[4096,512]{0,1:T(8,128)} %fusion.38), kind=kLoop, calls=%fused_computation.40 | loop fusion | flops 2621440 | bytes 20971520 | tf_op jit(solution)/shard_map/concatenate | solution.py:127
  289.4 17.9 %all_to_all.32 = bf16[8,128,512]{2,1,0:T(8,128)(2,1)S(1)} all-to-all(bf16[8,128,512]{2,1,0:T(8,128)(2,1)S(1)} %copy.112), channel_id=1, replica_groups=mesh['ctx'=8,'dp'=4] {'ctx'}, dimensions={0} | all-to-all | bytes 2097152 | tf_op jit(solution)/shard_map/all_to_all | solution.py:116
  309.3 156.5 %reduce-scatter.2.cloned.1.call-done = f32[1024,640]{0,1:T(8,128)} async-done(((f32[4096,640]{0,1:T(8,128)}), f32[1024,640]{0,1:T(8,128)}) %reduce-scatter.2.cloned.1.call-update) | async-done | bytes 2621456 | tf_op jit(solution)/shard_map/reduce_scatter | solution.py:126
  (116 shorter events, 44.5 us)
Async XLA Ops:
  7.2 111.6 %copy-start = (s32[4,8,8]{2,1,0:T(8,128)S(1)}, s32[4,8,8]{2,1,0:T(8,128)}, u32[]{:S(2)}) copy-start(s32[4,8,8]{2,1,0:T(8,128)} %param.12) | copy-start | bytes 3076
  7.2 105.2 %copy-start.12 = (bf16[1,128,4096]{2,1,0:T(8,128)(2,1)S(1)}, bf16[1,128,4096]{2,1,0:T(8,128)(2,1)}, u32[]{:S(2)}) copy-start(bf16[1,128,4096]{2,1,0:T(8,128)(2,1)} %param.11) | copy-start | bytes 3145732
  7.2 103.8 %all-gather.4.cloned.1.call-start = ((), (), s32[]{:S(2)}) async-start(), calls=%async_computation.3 | async-start | bytes 6553600 | tf_op jit(solution)/shard_map/all_gather | solution.py:89
  9.8 163.3 %all-gather.6.cloned.1.call-start = ((), (), s32[]{:S(2)}) async-start(), calls=%async_computation.5 | async-start | bytes 9437184 | tf_op jit(solution)/shard_map/all_gather | solution.py:94
  112.3 12.5 %collective-permute-start = (bf16[4096,128]{1,0:T(8,128)(2,1)S(1)}, bf16[4096,128]{1,0:T(8,128)(2,1)}, u32[]{:S(2)}, u32[]{:S(2)}) collective-permute-start(bf16[4096,128]{1,0:T(8,128)(2,1)S(1)} %slice.36), channel_id=1, source_target_pairs={{0,4},{4,0},{8,12},{12,8},{16,20},{20,16},{24,28},{28,24},{1,5},{5... | collective-permute-start | bytes 3145736 | tf_op jit(solution)/shard_map/ppermute | solution.py:14
  113.6 71.9 %all-to-all-start = ((bf16[128,8,512]{0,2,1:T(8,128)(2,1)}), bf16[128,8,512]{0,2,1:T(8,128)(2,1)}, u32[]{:S(2)}, u32[]{:S(2)}) async-start(bf16[128,8,512]{0,2,1:T(8,128)(2,1)} %bitcast.39), calls=%async_computation | async-start | bytes 2097152 | tf_op jit(solution)/shard_map/all_to_all | solution.py:111
  117.9 347.9 %reduce-scatter.2.cloned.1.call-start = ((), (), s32[]{:S(2)}) async-start(), calls=%async_computation.4 | async-start | bytes 13107200 | tf_op jit(solution)/shard_map/reduce_scatter | solution.py:126
  185.6 65.5 %copy-start.14 = (s32[8,8]{0,1:T(8,128)S(1)}, s32[8,8]{0,1:T(8,128)}, u32[]{:S(2)}) copy-start(s32[8,8]{0,1:T(8,128)} %copy.76) | copy-start | bytes 772
  185.6 65.5 %copy-start.15 = (pred[8,8]{0,1:T(8,128)(4,1)S(1)}, pred[8,8]{0,1:T(8,128)(4,1)}, u32[]{:S(2)}) copy-start(pred[8,8]{0,1:T(8,128)(4,1)} %iota_compare_fusion.1) | copy-start | bytes 196
  189.5 8.4 %copy-start.2 = (f32[4,8,128,128,4]{3,2,4,1,0:T(8,128)}, f32[4,8,128,128,4]{3,2,4,1,0:T(8,128)S(1)}, u32[]{:S(2)}) copy-start(f32[4,8,128,128,4]{3,2,4,1,0:T(8,128)S(1)} %get-tuple-element.224) | copy-start | bytes 25165828 | tf_op jit(solution)/shard_map/while
  189.6 5.2 %copy-start.6 = (f32[2,4,8,128,128]{4,3,2,1,0:T(8,128)S(1)}, f32[2,4,8,128,128]{4,3,2,1,0:T(8,128)}, u32[]{:S(2)}) copy-start(f32[2,4,8,128,128]{4,3,2,1,0:T(8,128)} %get-tuple-element.244) | copy-start | bytes 12582916 | tf_op jit(solution)/shard_map/while
  200.7 7.8 %copy-start.3 = (f32[4,8,128,128,4]{3,2,4,1,0:T(8,128)S(1)}, f32[4,8,128,128,4]{3,2,4,1,0:T(8,128)}, u32[]{:S(2)}) copy-start(f32[4,8,128,128,4]{3,2,4,1,0:T(8,128)} %copy-done.2) | copy-start | bytes 25165828 | tf_op jit(solution)/shard_map/while
  208.4 4.4 copy-start.4
  212.8 4.4 copy-start.9
  222.2 8.4 %copy-start.2 = (f32[4,8,128,128,4]{3,2,4,1,0:T(8,128)}, f32[4,8,128,128,4]{3,2,4,1,0:T(8,128)S(1)}, u32[]{:S(2)}) copy-start(f32[4,8,128,128,4]{3,2,4,1,0:T(8,128)S(1)} %get-tuple-element.224) | copy-start | bytes 25165828 | tf_op jit(solution)/shard_map/while
  222.2 5.2 %copy-start.6 = (f32[2,4,8,128,128]{4,3,2,1,0:T(8,128)S(1)}, f32[2,4,8,128,128]{4,3,2,1,0:T(8,128)}, u32[]{:S(2)}) copy-start(f32[2,4,8,128,128]{4,3,2,1,0:T(8,128)} %get-tuple-element.244) | copy-start | bytes 12582916 | tf_op jit(solution)/shard_map/while
  233.3 7.8 %copy-start.3 = (f32[4,8,128,128,4]{3,2,4,1,0:T(8,128)S(1)}, f32[4,8,128,128,4]{3,2,4,1,0:T(8,128)}, u32[]{:S(2)}) copy-start(f32[4,8,128,128,4]{3,2,4,1,0:T(8,128)} %copy-done.2) | copy-start | bytes 25165828 | tf_op jit(solution)/shard_map/while
  241.1 4.4 copy-start.4
  245.4 4.4 copy-start.9
  251.1 7.4 %copy-start.8 = (f32[2,4,8,128,128]{4,3,2,1,0:T(8,128)S(1)}, f32[2,4,8,128,128]{4,3,2,1,0:T(8,128)}, u32[]{:S(2)}) copy-start(f32[2,4,8,128,128]{4,3,2,1,0:T(8,128)} %get-tuple-element.66) | copy-start | bytes 12582916
  258.3 5.6 %copy-start.11 = (bf16[2,4,128,4,128]{4,3,2,1,0:T(4,128)(2,1)S(1)}, bf16[2,4,128,4,128]{4,3,2,1,0:T(4,128)(2,1)}, u32[]{:S(2)}) copy-start(bf16[2,4,128,4,128]{4,3,2,1,0:T(4,128)(2,1)} %get-tuple-element.64) | copy-start | bytes 3145732
  263.6 10.5 %collective-permute-start.1 = (f32[1024,256]{1,0:T(8,128)S(1)}, f32[1024,256]{1,0:T(8,128)}, u32[]{:S(2)}, u32[]{:S(2)}) collective-permute-start(f32[1024,256]{1,0:T(8,128)S(1)} %pad_maximum_fusion.2), channel_id=1, source_target_pairs={{0,4},{4,0},{8,12},{12,8},{16,20},{20,16},{24,28},{28,24},{1,5},{5... | collective-permute-start | bytes 3145736 | tf_op jit(solution)/shard_map/ppermute | solution.py:14
  308.0 162.3 %copy-start.1 = (s32[4,8,8]{2,1,0:T(8,128)S(1)}, s32[4,8,8]{2,1,0:T(8,128)}, u32[]{:S(2)}) copy-start(s32[4,8,8]{2,1,0:T(8,128)} %param.12) | copy-start | bytes 3076
  465.8 3.4 slice-start.1
  (8 other events, 12.6 us)
Sparse Core Ops, SparseCore 0:
  10.2 100.7 all-gather.3
  112.8 60.2 all-gather.5
  287.8 178.0 reduce-scatter.1

commit v2 on v1

--- a/solution.py
+++ b/solution.py
@@ -82,6 +82,12 @@
 
 def shards(tokens, query_weight, keyval_matrix, grad_out, blocks, counts):
     local_rows = tokens[0]
+    dp_size = lax.axis_size("dp")
+    row_block = local_rows.shape[1] // dp_size
+    row_slices = lax.all_to_all(
+        local_rows.reshape(local_rows.shape[0], dp_size, row_block).transpose(1, 0, 2),
+        "dp", split_axis=0, concat_axis=0, tiled=True,
+    )
     group_size = lax.axis_size("ctx") // blocks.shape[0]
     group_bits = group_size.bit_length() - 1
     device = lax.axis_index("ctx")
@@ -120,11 +126,12 @@
     width = summed.shape[1] // group_size
     own_grad = lax.dynamic_slice_in_dim(summed, device % group_size * width, width, 1)
     own_grad = own_grad.astype(jnp.bfloat16)
-    contract = (((0,), (0,)), ((), ()))
-    grad_query = lax.dot_general(all_rows, dquery, contract, preferred_element_type=jnp.float32)
-    grad_keyval = lax.dot_general(all_rows, own_grad, contract, preferred_element_type=jnp.float32)
-    grads = lax.psum_scatter(
-        jnp.concatenate([grad_query, grad_keyval], axis=1), "dp", scatter_dimension=0, tiled=True
+    cotangents = lax.all_gather(
+        jnp.concatenate([dquery, own_grad], axis=1), "dp", axis=0, tiled=False
+    )
+    row_tokens = lax.all_gather(row_slices, "ctx", axis=1, tiled=True)
+    grads = jnp.einsum(
+        "spr,spk->rk", row_tokens, cotangents, preferred_element_type=jnp.float32
     )
     grad_query = grads[:, :query_cols]
     grad_keyval = grads[:, query_cols:]

time: 478 us -> 412 us (0.86)
  waiting for transfers between devices: 304 us -> 241 us
  starting transfers between devices: 4.76 us -> 11 us
  other arithmetic: 20.1 us -> 14.8 us
    reduce_scatter x1 -> x0, waiting for transfers between devices: 157 us -> none  [shards(): lax.psum_scatter(jnp.concatenate([grad_query, grad_keyval], axis=1), 'dp'...]
    all_gather x0 -> x2, waiting for transfers between devices: none -> 77.5 us  [the longest x1 77.5 us: shards(): lax.all_gather(jnp.concatenate([dquery, own_grad], axis=1), 'dp', axis=0,...]
    all_gather x1, waiting for transfers between devices: 100 us -> 111 us  [shards(): lax.all_gather(jnp.concatenate([query_weight, keyval_matrix], axis=1), 'd...]
    concatenate x1, other arithmetic: 8.64 us -> 1.17 us  [shards(): jnp.concatenate([dquery, own_grad], axis=1)]
    all_to_all x0 -> x1, starting transfers between devices: none -> 6.32 us  [shards(): lax.all_to_all(local_rows.reshape(local_rows.shape[0], dp_size, row_block...]
    dot_general x2 -> x1, matrix products: 15 us -> 9.58 us  [shards(): jnp.einsum('spr,spk->rk', row_tokens, cotangents, preferred_element_type=...]
  transfers between devices with their start and end apart: 6 -> 8, of which waited for: 3 -> 4; matrix products, arithmetic and copies ran while one was open for 8% -> 23% of each run, Pallas kernels for 0% -> 0%
where the time goes in v2:
time: 412 us
  waiting for transfers between devices  241 us (58%)
  matrix products  68.4 us (17%)
  local copies, waits for them, and re-layouts  44.4 us (11%)
  blocking collectives  17.8 us (4%)
  other arithmetic  14.8 us (4%)
  between operations  14 us (3%)
  starting transfers between devices  11 us (3%)
    all_gather x1, waiting for transfers between devices, shards(): lax.all_gather(jnp.concatenate([query_weight, keyval_matrix], axis=1), 'd...  111 us
    all_gather x1, waiting for transfers between devices, shards(): lax.all_gather(jnp.concatenate([dquery, own_grad], axis=1), 'dp', axis=0,...  77.5 us
    all_gather x1, waiting for transfers between devices, shards(): all_rows = lax.all_gather(local_rows, 'ctx', axis=0, tiled=True)  48.4 us
    all_to_all x1, blocking collectives, shards(): lax.all_to_all(out_heads, 'ctx', split_axis=0, concat_axis=1, tiled=True)  17.8 us
    while x32, local copies, waits for them, and re-layouts  17.1 us
    dot_general x2, matrix products, attend_part(): jnp.einsum('nhqkc,nkcd->nqhd', probs_b, vals, preferred_element_type=jnp....  14.4 us
    dot_general x1, matrix products, shards(): jnp.dot(all_rows, jnp.concatenate([query_full, keyval_cols], axis=1), pre...  10.4 us
    dot_general x1, matrix products, shards(): jnp.einsum('spr,spk->rk', row_tokens, cotangents, preferred_element_type=...  9.58 us
  transfers between devices with their start and end apart: 8, of which 4 were waited for; matrix products, arithmetic and copies ran while one was open for 23% of the time, Pallas kernels for 0%

profile of v2, /device:TPU:0, one launch (start us, length us, event | category | flops | bytes accessed | tf_op | source)
XLA Modules:
  0.0 411.5 jit_solution(13970860436636946497)
XLA Ops:
  7.2 2.6 pad_maximum_fusion
  12.6 6.3 %all-to-all-start.2 = ((bf16[4,128,1024]{2,1,0:T(8,128)(2,1)}), bf16[4,128,1024]{2,1,0:T(8,128)(2,1)S(1)}, u32[]{:S(2)}, u32[]{:S(2)}) async-start(bf16[4,128,1024]{2,1,0:T(8,128)(2,1)} %bitcast.58), calls=%async_computation.2 | async-start | bytes 2097152 | tf_op jit(solution)/shard_map/all_to_all | solution.py:87
  18.9 110.7 %all-gather.7.cloned.1.call-done = bf16[4096,640]{1,0:T(8,128)(2,1)} async-done(((bf16[1024,640]{1,0:T(8,128)(2,1)}), bf16[4096,640]{1,0:T(8,128)(2,1)}) %all-gather.7.cloned.1.call-update) | async-done | bytes 5242896 | tf_op jit(solution)/shard_map/all_gather | solution.py:95
  134.4 4.3 %all-to-all-start = ((bf16[128,8,512]{0,2,1:T(8,128)(2,1)}), bf16[128,8,512]{0,2,1:T(8,128)(2,1)}, u32[]{:S(2)}, u32[]{:S(2)}) async-start(bf16[128,8,512]{0,2,1:T(8,128)(2,1)} %bitcast.39), calls=%async_computation | async-start | bytes 2097152 | tf_op jit(solution)/shard_map/all_to_all | solution.py:117
  139.5 4.6 %slice.35 = bf16[4096,512]{1,0:T(8,128)(2,1)} slice(bf16[4096,640]{1,0:T(8,128)(2,1)} %all-gather.7.cloned.1.call-done), slice={[0:4096], [0:512]} | slice | bytes 8388608 | tf_op jit(solution)/shard_map/slice | solution.py:98
  144.1 2.1 maximum_select_fusion
  146.2 48.4 %all-gather.11.cloned.1.call-done = bf16[1,1024,4096]{2,1,0:T(8,128)(2,1)} async-done(((bf16[1,128,4096]{2,1,0:T(8,128)(2,1)}), bf16[1,1024,4096]{2,1,0:T(8,128)(2,1)}) %all-gather.11.cloned.1.call-update) | async-done | bytes 8388624 | tf_op jit(solution)/shard_map/all_gather | solution.py:100
  194.6 10.4 %fusion.46 = bf16[1024,768]{0,1:T(8,128)(2,1)S(1)} fusion(bf16[1,1024,4096]{2,1,0:T(8,128)(2,1)} %all-gather.11.cloned.1.call-done, bf16[4096,256]{1,0:T(8,128)(2,1)S(1)} %maximum_select_fusion, bf16[4096,512]{1,0:T(8,128)(2,1)} %slice.35), kind=kOutput, calls=%fused_computation.52 | convolution fusion | flops 6455820288 | bytes 16252928 | tf_op jit(solution)/shard_map/dot_general | solution.py:110
  207.1 67.3 %while.16 = (s32[]{:T(128)}, bf16[2,4,128,4,128]{2,4,3,1,0:T(8,128)(2,1)}, bf16[2,4,128,4,128]{4,3,2,1,0:T(4,128)(2,1)}, f32[2,4,8,128,128]{4,3,2,1,0:T(8,128)},...) while((s32[]{:T(128)}, ...), condition=%wide.region_4.5_spmd, body=%wide.region_0.4_spmd.sunk | while | flops 3275222016 | bytes 218726320 | solution.py:62
  212.9 2.4 copy-done.2
  216.3 3.2 bitcast_dynamic-update-slice_fusion.8
  219.5 2.1 copy-done.7
  222.3 7.8 %bitcast_dynamic-update-slice_fusion.6 = (bf16[2,4,128,4,128]{2,4,3,1,0:T(8,128)(2,1)}, bf16[4,128,4,128]{3,1,2,0:T(8,128)(2,1)S(1)}) fusion(bf16[2,4,128,4,128]{2,4,3,1,0:T(8,128)(2,1)} %get-tuple-element.241, s32[]{:T(128)} %get-tuple-element.240, bf16[4,8,128,128,1]{3,2,4,1,0:T(8,128)(2,1)S(1)} %bitcast.228, f32[4,4,128]{2,1,0:T(4,128)S(1)} %fusion.106, ...), kind=kOutput, calls=%fused_computation.26.clone.1 | convolution fusion | flops 547618816 | bytes 10502688 | tf_op jit(solution)/shard_map/while/body/eval_jaxpr/nhqkc,nkcd->nqhd/dot_general | solution.py:27
  231.4 4.3 %fusion.107 = bf16[4,4,128,8,128]{2,4,1,3,0:T(8,128)(2,1)S(1)} fusion(f32[4,4,128]{2,1,0:T(4,128)S(1)} %bitcast.241, bf16[4,8,128,128,1]{3,2,4,1,0:T(8,128)(2,1)S(1)} %bitcast.229, bf16[2,4,128,4,128]{2,4,3,1,0:T(8,128)(2,1)} %get-tuple-element.262, s32[]{:T(128)} %get-tuple-element.240, f32[4,4,128]{2,1,0:T(4,128)S(1)} %fusion.106, ...), kind=kOutput, calls=%fused_computation.5.clone.1 | convolution fusion | flops 553648128 | bytes 14180896 | tf_op jit(solution)/shard_map/while/body/eval_jaxpr/nqhd,nkcd->nhqkc/dot_general | solution.py:33
  247.1 2.4 copy-done.2
  250.5 3.2 bitcast_dynamic-update-slice_fusion.8
  256.6 6.5 %bitcast_dynamic-update-slice_fusion.6 = (bf16[2,4,128,4,128]{2,4,3,1,0:T(8,128)(2,1)}, bf16[4,128,4,128]{3,1,2,0:T(8,128)(2,1)S(1)}) fusion(bf16[2,4,128,4,128]{2,4,3,1,0:T(8,128)(2,1)} %get-tuple-element.241, s32[]{:T(128)} %get-tuple-element.240, bf16[4,8,128,128,1]{3,2,4,1,0:T(8,128)(2,1)S(1)} %bitcast.228, f32[4,4,128]{2,1,0:T(4,128)S(1)} %fusion.106, ...), kind=kOutput, calls=%fused_computation.26.clone.1 | convolution fusion | flops 547618816 | bytes 10502688 | tf_op jit(solution)/shard_map/while/body/eval_jaxpr/nhqkc,nkcd->nqhd/dot_general | solution.py:27
  264.3 4.3 %fusion.107 = bf16[4,4,128,8,128]{2,4,1,3,0:T(8,128)(2,1)S(1)} fusion(f32[4,4,128]{2,1,0:T(4,128)S(1)} %bitcast.241, bf16[4,8,128,128,1]{3,2,4,1,0:T(8,128)(2,1)S(1)} %bitcast.229, bf16[2,4,128,4,128]{2,4,3,1,0:T(8,128)(2,1)} %get-tuple-element.262, s32[]{:T(128)} %get-tuple-element.240, f32[4,4,128]{2,1,0:T(4,128)S(1)} %fusion.106, ...), kind=kOutput, calls=%fused_computation.5.clone.1 | convolution fusion | flops 553648128 | bytes 14180896 | tf_op jit(solution)/shard_map/while/body/eval_jaxpr/nqhd,nkcd->nhqkc/dot_general | solution.py:33
  274.4 7.2 %fusion.51 = f32[8,128,128]{2,0,1:T(8,128)S(1)} fusion(f32[8,8,128,128]{3,2,1,0:T(8,128)} %bitcast.234, s32[8,8]{0,1:T(8,128)S(1)} %copy-done.17, pred[8,8]{0,1:T(8,128)(4,1)S(1)} %copy-done.18), kind=kOutput, calls=%fused_computation.58 | convolution fusion | flops 100664320 | bytes 4718912 | tf_op jit(solution)/shard_map/bnk,nkcd->bcd/dot_general | solution.py:71
  281.8 5.0 %fusion.54 = f32[8,128,128]{2,0,1:T(8,128)S(1)} fusion(f32[8,8,128,128]{3,2,1,0:T(8,128)S(1)} %bitcast.235, s32[8,8]{0,1:T(8,128)S(1)} %copy-done.17, pred[8,8]{0,1:T(8,128)(4,1)S(1)} %copy-done.18), kind=kOutput, calls=%fused_computation.59 | convolution fusion | flops 100664320 | bytes 4718912 | tf_op jit(solution)/shard_map/bnk,nkcd->bcd/dot_general | solution.py:72
  288.3 2.7 collective-permute-done.1
  293.9 17.8 %all_to_all.37 = bf16[8,128,512]{2,1,0:T(8,128)(2,1)S(1)} all-to-all(bf16[8,128,512]{2,1,0:T(8,128)(2,1)S(1)} %copy.122), channel_id=1, replica_groups=mesh['ctx'=8,'dp'=4] {'ctx'}, dimensions={0} | all-to-all | bytes 2097152 | tf_op jit(solution)/shard_map/all_to_all | solution.py:122
  313.6 77.5 %all-gather.13.cloned.1.call-done = bf16[4096,640]{1,0:T(8,128)(2,1)} async-done(((bf16[1024,640]{1,0:T(8,128)(2,1)}), bf16[4096,640]{1,0:T(8,128)(2,1)}) %all-gather.13.cloned.1.call-update) | async-done | bytes 5242896 | tf_op jit(solution)/shard_map/all_gather | solution.py:129
  391.1 9.6 %convolution_bitcast_fusion.1 = f32[1024,640]{0,1:T(8,128)S(1)} fusion(bf16[4,1024,640]{2,1,0:T(8,128)(2,1)} %bitcast.243, bf16[4,1024,1024]{2,1,0:T(8,128)(2,1)} %all-gather.9.cloned.1.call-done), kind=kOutput, calls=%fused_computation.50 | convolution fusion | flops 5368709120 | bytes 16252928 | tf_op jit(solution)/shard_map/spr,spk->rk/dot_general | solution.py:133
  (129 shorter events, 51.6 us)
Async XLA Ops:
  7.2 126.0 %copy-start = (s32[4,8,8]{2,1,0:T(8,128)S(1)}, s32[4,8,8]{2,1,0:T(8,128)}, u32[]{:S(2)}) copy-start(s32[4,8,8]{2,1,0:T(8,128)} %param.12) | copy-start | bytes 3076
  7.2 122.4 %all-gather.7.cloned.1.call-start = ((), (), s32[]{:S(2)}) async-start(), calls=%async_computation.3 | async-start | bytes 6553600 | tf_op jit(solution)/shard_map/all_gather | solution.py:95
  9.8 184.8 %all-gather.11.cloned.1.call-start = ((), (), s32[]{:S(2)}) async-start(), calls=%async_computation.5 | async-start | bytes 9437184 | tf_op jit(solution)/shard_map/all_gather | solution.py:100
  10.6 121.3 %copy-start.12 = (bf16[1,128,4096]{2,1,0:T(8,128)(2,1)S(1)}, bf16[1,128,4096]{2,1,0:T(8,128)(2,1)}, u32[]{:S(2)}) copy-start(bf16[1,128,4096]{2,1,0:T(8,128)(2,1)} %param.11) | copy-start | bytes 3145732
  12.6 121.8 %all-to-all-start.2 = ((bf16[4,128,1024]{2,1,0:T(8,128)(2,1)}), bf16[4,128,1024]{2,1,0:T(8,128)(2,1)S(1)}, u32[]{:S(2)}, u32[]{:S(2)}) async-start(bf16[4,128,1024]{2,1,0:T(8,128)(2,1)} %bitcast.58), calls=%async_computation.2 | async-start | bytes 2097152 | tf_op jit(solution)/shard_map/all_to_all | solution.py:87
  130.9 13.2 %collective-permute-start = (bf16[4096,128]{1,0:T(8,128)(2,1)S(1)}, bf16[4096,128]{1,0:T(8,128)(2,1)}, u32[]{:S(2)}, u32[]{:S(2)}) collective-permute-start(bf16[4096,128]{1,0:T(8,128)(2,1)S(1)} %slice.36), channel_id=1, source_target_pairs={{0,4},{4,0},{8,12},{12,8},{16,20},{20,16},{24,28},{28,24},{1,5},{5... | collective-permute-start | bytes 3145736 | tf_op jit(solution)/shard_map/ppermute | solution.py:14
  134.4 4.3 %copy-start.10 = (bf16[4,128,1024]{2,1,0:T(8,128)(2,1)}, bf16[4,128,1024]{2,1,0:T(8,128)(2,1)S(1)}, u32[]{:S(2)}) copy-start(bf16[4,128,1024]{2,1,0:T(8,128)(2,1)S(1)} %all-to-all-done.2) | copy-start | bytes 3145732
  134.4 72.7 %all-to-all-start = ((bf16[128,8,512]{0,2,1:T(8,128)(2,1)}), bf16[128,8,512]{0,2,1:T(8,128)(2,1)}, u32[]{:S(2)}, u32[]{:S(2)}) async-start(bf16[128,8,512]{0,2,1:T(8,128)(2,1)} %bitcast.39), calls=%async_computation | async-start | bytes 2097152 | tf_op jit(solution)/shard_map/all_to_all | solution.py:117
  138.7 174.9 %all-gather.9.cloned.1.call-start = ((), (), s32[]{:S(2)}) async-start(), calls=%async_computation.4 | async-start | bytes 9437184 | tf_op jit(solution)/shard_map/all_gather | solution.py:132
  139.4 251.7 %all-gather.13.cloned.1.call-start = ((), (), s32[]{:S(2)}) async-start(), calls=%async_computation.6 | async-start | bytes 6553600 | tf_op jit(solution)/shard_map/all_gather | solution.py:129
  207.1 67.3 %copy-start.17 = (s32[8,8]{0,1:T(8,128)S(1)}, s32[8,8]{0,1:T(8,128)}, u32[]{:S(2)}) copy-start(s32[8,8]{0,1:T(8,128)} %copy.82) | copy-start | bytes 772
  207.1 67.3 %copy-start.18 = (pred[8,8]{0,1:T(8,128)(4,1)S(1)}, pred[8,8]{0,1:T(8,128)(4,1)}, u32[]{:S(2)}) copy-start(pred[8,8]{0,1:T(8,128)(4,1)} %iota_compare_fusion.1) | copy-start | bytes 196
  211.1 5.2 %copy-start.6 = (f32[2,4,8,128,128]{4,3,2,1,0:T(8,128)S(1)}, f32[2,4,8,128,128]{4,3,2,1,0:T(8,128)}, u32[]{:S(2)}) copy-start(f32[2,4,8,128,128]{4,3,2,1,0:T(8,128)} %get-tuple-element.244) | copy-start | bytes 12582916 | tf_op jit(solution)/shard_map/while
  222.3 9.1 %copy-start.3 = (f32[4,8,128,128,4]{3,2,4,1,0:T(8,128)S(1)}, f32[4,8,128,128,4]{3,2,4,1,0:T(8,128)}, u32[]{:S(2)}) copy-start(f32[4,8,128,128,4]{3,2,4,1,0:T(8,128)} %copy-done.2) | copy-start | bytes 25165828 | tf_op jit(solution)/shard_map/while
  231.4 4.4 %copy-start.4 = (f32[2,4,8,128,128]{4,3,2,1,0:T(8,128)S(1)}, f32[2,4,8,128,128]{4,3,2,1,0:T(8,128)}, u32[]{:S(2)}) copy-start(f32[2,4,8,128,128]{4,3,2,1,0:T(8,128)} %get-tuple-element.243) | copy-start | bytes 12582916 | tf_op jit(solution)/shard_map/while
  245.2 4.3 %copy-start.2 = (f32[4,8,128,128,4]{3,2,4,1,0:T(8,128)}, f32[4,8,128,128,4]{3,2,4,1,0:T(8,128)S(1)}, u32[]{:S(2)}) copy-start(f32[4,8,128,128,4]{3,2,4,1,0:T(8,128)S(1)} %get-tuple-element.224) | copy-start | bytes 25165828 | tf_op jit(solution)/shard_map/while
  245.2 5.3 %copy-start.6 = (f32[2,4,8,128,128]{4,3,2,1,0:T(8,128)S(1)}, f32[2,4,8,128,128]{4,3,2,1,0:T(8,128)}, u32[]{:S(2)}) copy-start(f32[2,4,8,128,128]{4,3,2,1,0:T(8,128)} %get-tuple-element.244) | copy-start | bytes 12582916 | tf_op jit(solution)/shard_map/while
  256.5 7.8 %copy-start.3 = (f32[4,8,128,128,4]{3,2,4,1,0:T(8,128)S(1)}, f32[4,8,128,128,4]{3,2,4,1,0:T(8,128)}, u32[]{:S(2)}) copy-start(f32[4,8,128,128,4]{3,2,4,1,0:T(8,128)} %copy-done.2) | copy-start | bytes 25165828 | tf_op jit(solution)/shard_map/while
  264.3 4.4 %copy-start.4 = (f32[2,4,8,128,128]{4,3,2,1,0:T(8,128)S(1)}, f32[2,4,8,128,128]{4,3,2,1,0:T(8,128)}, u32[]{:S(2)}) copy-start(f32[2,4,8,128,128]{4,3,2,1,0:T(8,128)} %get-tuple-element.243) | copy-start | bytes 12582916 | tf_op jit(solution)/shard_map/while
  274.4 7.4 %copy-start.8 = (f32[2,4,8,128,128]{4,3,2,1,0:T(8,128)S(1)}, f32[2,4,8,128,128]{4,3,2,1,0:T(8,128)}, u32[]{:S(2)}) copy-start(f32[2,4,8,128,128]{4,3,2,1,0:T(8,128)} %get-tuple-element.66) | copy-start | bytes 12582916
  281.7 6.4 %copy-start.16 = (bf16[2,4,128,4,128]{4,3,2,1,0:T(4,128)(2,1)S(1)}, bf16[2,4,128,4,128]{4,3,2,1,0:T(4,128)(2,1)}, u32[]{:S(2)}) copy-start(bf16[2,4,128,4,128]{4,3,2,1,0:T(4,128)(2,1)} %get-tuple-element.64) | copy-start | bytes 3145732
  288.0 5.3 %copy-start.13 = (bf16[2,4,128,4,128]{2,4,3,1,0:T(8,128)(2,1)S(1)}, bf16[2,4,128,4,128]{2,4,3,1,0:T(8,128)(2,1)}, u32[]{:S(2)}) copy-start(bf16[2,4,128,4,128]{2,4,3,1,0:T(8,128)(2,1)} %get-tuple-element.63) | copy-start | bytes 3145732
  288.0 3.0 collective-permute-start.1
  400.7 4.3 %copy-start.1 = (s32[4,8,8]{2,1,0:T(8,128)S(1)}, s32[4,8,8]{2,1,0:T(8,128)}, u32[]{:S(2)}) copy-start(s32[4,8,8]{2,1,0:T(8,128)} %param.12) | copy-start | bytes 3076
  (12 other events, 23.6 us)
Sparse Core Ops, SparseCore 0:
  10.2 119.3 all-gather.6
  131.5 63.0 all-gather.10
  196.5 54.3 all-gather.8
  293.4 97.6 all-gather.12

commit v3 on v2

--- a/solution.py
+++ b/solution.py
@@ -80,6 +80,27 @@
     )
 
 
+def exchange_gather(block, axis, order):
+    count = lax.axis_size(axis)
+    held = block[None]
+    for bit in order:
+        held = jnp.concatenate([held, partner(held, axis, bit)], axis=0)
+    wanted = lax.broadcasted_iota(jnp.int32, (count,), 0) ^ lax.axis_index(axis)
+    slot = jnp.zeros((count,), jnp.int32)
+    for place, bit in enumerate(order):
+        slot = slot | ((wanted >> bit) & 1) << place
+    return jnp.take(held, slot, axis=0, mode="clip")
+
+
+def gather_rows(rows, axis):
+    bits = lax.axis_size(axis).bit_length() - 1
+    upper = list(range(1, bits))
+    half = rows.shape[0] // 2
+    first = exchange_gather(rows[:half], axis, upper + [0] if bits else [])
+    second = exchange_gather(rows[half:], axis, upper[::-1] + [0] if bits else [])
+    return jnp.concatenate([first, second], axis=1).reshape((-1,) + rows.shape[1:])
+
+
 def shards(tokens, query_weight, keyval_matrix, grad_out, blocks, counts):
     local_rows = tokens[0]
     dp_size = lax.axis_size("dp")
@@ -97,7 +118,7 @@
     )
     query_full = weights_full[:, :query_cols]
     keyval_part = weights_full[:, query_cols:]
-    all_rows = lax.all_gather(local_rows, "ctx", axis=0, tiled=True)
+    all_rows = gather_rows(local_rows, "ctx")
     keyval_cols = keyval_part
     for bit in range(group_bits):
         other = partner(keyval_cols, "ctx", bit)

time: 412 us -> 368 us (0.89)
  waiting for transfers between devices: 241 us -> 160 us
  other arithmetic: 14.8 us -> 36.2 us
  local copies, waits for them, and re-layouts: 44.4 us -> 58.7 us
  matrix products: 68.4 us -> 61.4 us
  starting transfers between devices: 11 us -> 17.2 us
    all_gather x1, waiting for transfers between devices: 111 us -> 6.24 us  [shards(): lax.all_gather(jnp.concatenate([query_weight, keyval_matrix], axis=1), 'd...]
    all_gather x1 -> x0, waiting for transfers between devices: 48.4 us -> none  [shards(): all_rows = lax.all_gather(local_rows, 'ctx', axis=0, tiled=True)]
    all_to_all x1, waiting for transfers between devices: 0.01 us -> 44.9 us  [shards(): lax.all_to_all(local_rows.reshape(local_rows.shape[0], dp_size, row_block...]
    ppermute x2 -> x8, waiting for transfers between devices: 2.69 us -> 32.9 us  [partner(): return lax.ppermute(block, axis, route)]
    concatenate x0 -> x7, other arithmetic: none -> 20.5 us  [the longest x6 12.7 us: exchange_gather(): held = jnp.concatenate([held, partner(held, axis, bit)], axis=0)]
    gather x0 -> x2, local copies, waits for them, and re-layouts: none -> 10.4 us  [exchange_gather(): return jnp.take(held, slot, axis=0, mode='clip')]
    ppermute x2 -> x8, starting transfers between devices: 0.25 us -> 8.53 us  [partner(): return lax.ppermute(block, axis, route)]
    unnamed x27 -> x31, local copies, waits for them, and re-layouts: 6.35 us -> 11.7 us
  transfers between devices with their start and end apart: 8 -> 13, of which waited for: 4 -> 6; matrix products, arithmetic and copies ran while one was open for 23% -> 32% of each run, Pallas kernels for 0% -> 0%
where the time goes in v3:
time: 368 us; the launch traced here: 367 us
  waiting for transfers between devices  160 us (43%)
  matrix products  61.4 us (17%)
  local copies, waits for them, and re-layouts  58.7 us (16%)
  other arithmetic  36.2 us (10%)
  blocking collectives  18.9 us (5%)
  starting transfers between devices  17.2 us (5%)
  between operations  14 us (4%)
    all_gather x1, waiting for transfers between devices, shards(): lax.all_gather(jnp.concatenate([dquery, own_grad], axis=1), 'dp', axis=0,...  75 us
    all_to_all x1, waiting for transfers between devices, shards(): lax.all_to_all(local_rows.reshape(local_rows.shape[0], dp_size, row_block...  44.9 us
    ppermute x8, waiting for transfers between devices, partner(): return lax.ppermute(block, axis, route)  32.9 us
    all_to_all x1, blocking collectives, shards(): lax.all_to_all(out_heads, 'ctx', split_axis=0, concat_axis=1, tiled=True)  18.9 us
    while x32, local copies, waits for them, and re-layouts  14.9 us
    dot_general x2, matrix products, attend_part(): jnp.einsum('nhqkc,nkcd->nqhd', probs_b, vals, preferred_element_type=jnp....  13.1 us
    concatenate x6, other arithmetic, exchange_gather(): held = jnp.concatenate([held, partner(held, axis, bit)], axis=0)  12.7 us
    unnamed x31, local copies, waits for them, and re-layouts  11.7 us
  transfers between devices with their start and end apart: 13, of which 6 were waited for; matrix products, arithmetic and copies ran while one was open for 32% of the time, Pallas kernels for 0%

profile of v3, /device:TPU:0, one launch (start us, length us, event | category | flops | bytes accessed | tf_op | source)
XLA Modules:
  0.0 366.7 jit_solution(1488545523227973213)
XLA Ops:
  9.9 3.0 collective-permute-start
  14.4 10.4 %collective-permute-done = bf16[1,64,4096]{2,1,0:T(8,128)(2,1)S(1)} collective-permute-done((bf16[1,64,4096]{2,1,0:T(8,128)(2,1)S(1)}, bf16[1,64,4096]{2,1,0:T(8,128)(2,1)S(1)}, u32[]{:S(2)}, u32[]{:S(2)}) %collective-permute-start) | collective-permute-done | bytes 524320 | tf_op jit(solution)/shard_map/ppermute | solution.py:14
  29.3 20.0 %collective-permute-done.1 = bf16[2,64,4096]{2,1,0:T(8,128)(2,1)S(1)} collective-permute-done((bf16[2,64,4096]{2,1,0:T(8,128)(2,1)S(1)}, bf16[2,64,4096]{2,1,0:T(8,128)(2,1)S(1)}, u32[]{:S(2)}, u32[]{:S(2)}) %collective-permute-start.1) | collective-permute-done | bytes 1048608 | tf_op jit(solution)/shard_map/ppermute | solution.py:14
  55.5 4.9 %all-to-all-start.2 = ((bf16[4,128,1024]{2,1,0:T(8,128)(2,1)}), bf16[4,128,1024]{2,1,0:T(8,128)(2,1)S(1)}, u32[]{:S(2)}, u32[]{:S(2)}) async-start(bf16[4,128,1024]{2,1,0:T(8,128)(2,1)} %bitcast.233), calls=%async_computation.2 | async-start | bytes 2097152 | tf_op jit(solution)/shard_map/all_to_all | solution.py:108
  67.8 44.9 %all-to-all-done.2 = bf16[4,128,1024]{2,1,0:T(8,128)(2,1)S(1)} async-done(((bf16[4,128,1024]{2,1,0:T(8,128)(2,1)}), bf16[4,128,1024]{2,1,0:T(8,128)(2,1)S(1)}, u32[]{:S(2)}, u32[]{:S(2)}) %all-to-all-start.2) | async-done | bytes 1048608 | tf_op jit(solution)/shard_map/all_to_all | solution.py:108
  113.7 3.7 %all-to-all-start = ((bf16[128,8,512]{0,2,1:T(8,128)(2,1)}), bf16[128,8,512]{0,2,1:T(8,128)(2,1)S(1)}, u32[]{:S(2)}, u32[]{:S(2)}) async-start(bf16[128,8,512]{0,2,1:T(8,128)(2,1)} %bitcast.232), calls=%async_computation | async-start | bytes 2097152 | tf_op jit(solution)/shard_map/all_to_all | solution.py:138
  118.2 3.6 pad_maximum_fusion.1
  121.8 4.9 %gather_fusion.2 = bf16[8,64,4096]{2,1,0:T(8,128)(2,1)} fusion(bf16[8,64,4096]{2,1,0:T(8,128)(2,1)} %pad_maximum_fusion.1, s32[1024]{0:T(1024)S(1)} %pad_clamp_fusion.2), kind=kCustom, calls=%fused_computation.2 | custom fusion | bytes 8388640 | tf_op jit(solution)/shard_map/jit(_take)/gather | solution.py:92
  126.7 6.2 %all-gather.5.cloned.1.call-done = bf16[4096,640]{1,0:T(8,128)(2,1)} async-done(((bf16[1024,640]{1,0:T(8,128)(2,1)}), bf16[4096,640]{1,0:T(8,128)(2,1)}) %all-gather.5.cloned.1.call-update) | async-done | bytes 5242896 | tf_op jit(solution)/shard_map/all_gather | solution.py:116
  135.3 3.6 pad_maximum_fusion.2
  138.9 5.5 %gather_fusion.3 = bf16[8,64,4096]{2,1,0:T(8,128)(2,1)} fusion(bf16[8,64,4096]{2,1,0:T(8,128)(2,1)} %pad_maximum_fusion.2, s32[1024]{0:T(1024)S(1)} %pad_clamp_fusion.1), kind=kCustom, calls=%fused_computation.3 | custom fusion | bytes 8388640 | tf_op jit(solution)/shard_map/jit(_take)/gather | solution.py:92
  144.3 7.8 %pad_maximum_fusion = bf16[8,128,4096]{2,1,0:T(8,128)(2,1)} fusion(bf16[8,64,4096]{2,1,0:T(8,128)(2,1)} %gather_fusion.3, bf16[8,64,4096]{2,1,0:T(8,128)(2,1)} %gather_fusion.2), kind=kLoop, calls=%fused_computation.41 | loop fusion | flops 16777216 | bytes 16777216 | tf_op jit(solution)/shard_map/concatenate | solution.py:101
  152.2 2.9 maximum_select_fusion
  158.0 6.6 %fusion.38 = bf16[1024,768]{1,0:T(8,128)(2,1)S(1)} fusion(bf16[1024,4096]{1,0:T(8,128)(2,1)S(1)} %bitcast.225, bf16[4096,256]{1,0:T(8,128)(2,1)S(1)} %maximum_select_fusion, bf16[4096,512]{1,0:T(8,128)(2,1)S(1)} %slice-done), kind=kOutput, calls=%fused_computation.56 | convolution fusion | flops 6455820288 | bytes 16252928 | tf_op jit(solution)/shard_map/dot_general | solution.py:131
  168.1 62.8 %while.16 = (s32[]{:T(128)}, bf16[2,4,128,4,128]{2,4,3,1,0:T(8,128)(2,1)}, bf16[2,4,128,4,128]{4,3,2,1,0:T(4,128)(2,1)}, f32[2,4,8,128,128]{4,3,2,1,0:T(8,128)},...) while((s32[]{:T(128)}, ...), condition=%wide.region_4.5_spmd, body=%wide.region_0.4_spmd.sunk | while | flops 3275222016 | bytes 217678256 | solution.py:62
  182.1 6.6 %bitcast_dynamic-update-slice_fusion.6 = (bf16[2,4,128,4,128]{2,4,3,1,0:T(8,128)(2,1)}, bf16[4,128,4,128]{3,1,2,0:T(8,128)(2,1)S(1)}) fusion(bf16[2,4,128,4,128]{2,4,3,1,0:T(8,128)(2,1)} %get-tuple-element.243, s32[]{:T(128)} %get-tuple-element.242, bf16[4,8,128,128,1]{3,2,4,1,0:T(8,128)(2,1)S(1)} %bitcast.222, f32[4,4,128]{2,1,0:T(4,128)S(1)} %fusion.96, ...), kind=kOutput, calls=%fused_computation.29.clone.1 | convolution fusion | flops 547618816 | bytes 10502688 | tf_op jit(solution)/shard_map/while/body/eval_jaxpr/nhqkc,nkcd->nqhd/dot_general | solution.py:27
  189.9 4.3 %fusion.97 = bf16[4,4,128,8,128]{2,4,1,3,0:T(8,128)(2,1)S(1)} fusion(f32[4,4,128]{2,1,0:T(4,128)S(1)} %bitcast.239, bf16[4,8,128,128,1]{3,2,4,1,0:T(8,128)(2,1)S(1)} %bitcast.223, bf16[2,4,128,4,128]{2,4,3,1,0:T(8,128)(2,1)} %copy-done.4, s32[]{:T(128)} %get-tuple-element.242, f32[4,4,128]{2,1,0:T(4,128)S(1)} %fusion.96, ...), kind=kOutput, calls=%fused_computation.7.clone.1 | convolution fusion | flops 553648128 | bytes 14180896 | tf_op jit(solution)/shard_map/while/body/eval_jaxpr/nqhd,nkcd->nhqkc/dot_general | solution.py:33
  213.3 6.5 %bitcast_dynamic-update-slice_fusion.6 = (bf16[2,4,128,4,128]{2,4,3,1,0:T(8,128)(2,1)}, bf16[4,128,4,128]{3,1,2,0:T(8,128)(2,1)S(1)}) fusion(bf16[2,4,128,4,128]{2,4,3,1,0:T(8,128)(2,1)} %get-tuple-element.243, s32[]{:T(128)} %get-tuple-element.242, bf16[4,8,128,128,1]{3,2,4,1,0:T(8,128)(2,1)S(1)} %bitcast.222, f32[4,4,128]{2,1,0:T(4,128)S(1)} %fusion.96, ...), kind=kOutput, calls=%fused_computation.29.clone.1 | convolution fusion | flops 547618816 | bytes 10502688 | tf_op jit(solution)/shard_map/while/body/eval_jaxpr/nhqkc,nkcd->nqhd/dot_general | solution.py:27
  221.1 4.3 %fusion.97 = bf16[4,4,128,8,128]{2,4,1,3,0:T(8,128)(2,1)S(1)} fusion(f32[4,4,128]{2,1,0:T(4,128)S(1)} %bitcast.239, bf16[4,8,128,128,1]{3,2,4,1,0:T(8,128)(2,1)S(1)} %bitcast.223, bf16[2,4,128,4,128]{2,4,3,1,0:T(8,128)(2,1)} %copy-done.4, s32[]{:T(128)} %get-tuple-element.242, f32[4,4,128]{2,1,0:T(4,128)S(1)} %fusion.96, ...), kind=kOutput, calls=%fused_computation.7.clone.1 | convolution fusion | flops 553648128 | bytes 14180896 | tf_op jit(solution)/shard_map/while/body/eval_jaxpr/nqhd,nkcd->nhqkc/dot_general | solution.py:33
  230.9 7.2 %fusion.41 = f32[8,128,128]{2,0,1:T(8,128)S(1)} fusion(f32[8,8,128,128]{3,2,1,0:T(8,128)} %bitcast.230, s32[8,8]{0,1:T(8,128)S(1)} %copy-done.19, pred[8,8]{0,1:T(8,128)(4,1)S(1)} %copy-done.20), kind=kOutput, calls=%fused_computation.62 | convolution fusion | flops 100664320 | bytes 4718912 | tf_op jit(solution)/shard_map/bnk,nkcd->bcd/dot_general | solution.py:71
  238.3 5.0 %fusion.44 = f32[8,128,128]{2,0,1:T(8,128)S(1)} fusion(f32[8,8,128,128]{3,2,1,0:T(8,128)S(1)} %bitcast.231, s32[8,8]{0,1:T(8,128)S(1)} %copy-done.19, pred[8,8]{0,1:T(8,128)(4,1)S(1)} %copy-done.20), kind=kOutput, calls=%fused_computation.63 | convolution fusion | flops 100664320 | bytes 4718912 | tf_op jit(solution)/shard_map/bnk,nkcd->bcd/dot_general | solution.py:72
  250.4 18.9 %all_to_all.37 = bf16[8,128,512]{2,1,0:T(8,128)(2,1)S(1)} all-to-all(bf16[8,128,512]{2,1,0:T(8,128)(2,1)S(1)} %copy.112), channel_id=1, replica_groups=mesh['ctx'=8,'dp'=4] {'ctx'}, dimensions={0} | all-to-all | bytes 2097152 | tf_op jit(solution)/shard_map/all_to_all | solution.py:143
  271.3 75.0 %all-gather.9.cloned.1.call-done = bf16[4096,640]{1,0:T(8,128)(2,1)} async-done(((bf16[1024,640]{1,0:T(8,128)(2,1)}), bf16[4096,640]{1,0:T(8,128)(2,1)}) %all-gather.9.cloned.1.call-update) | async-done | bytes 5242896 | tf_op jit(solution)/shard_map/all_gather | solution.py:150
  346.3 9.6 %convolution_bitcast_fusion.1 = f32[1024,640]{0,1:T(8,128)S(1)} fusion(bf16[4,1024,640]{2,1,0:T(8,128)(2,1)} %bitcast.241, bf16[4,1024,1024]{2,1,0:T(8,128)(2,1)} %all-gather.7.cloned.1.call-done), kind=kOutput, calls=%fused_computation.55 | convolution fusion | flops 5368709120 | bytes 16252928 | tf_op jit(solution)/shard_map/spr,spk->rk/dot_general | solution.py:154
  (153 shorter events, 86.5 us)
Async XLA Ops:
  7.2 59.3 %copy-start = (s32[4,8,8]{2,1,0:T(8,128)S(1)}, s32[4,8,8]{2,1,0:T(8,128)}, u32[]{:S(2)}) copy-start(s32[4,8,8]{2,1,0:T(8,128)} %param.12) | copy-start | bytes 3076
  7.2 125.8 %all-gather.5.cloned.1.call-start = ((), (), s32[]{:S(2)}) async-start(), calls=%async_computation.3 | async-start | bytes 6553600 | tf_op jit(solution)/shard_map/all_gather | solution.py:116
  9.9 14.9 %collective-permute-start = (bf16[1,64,4096]{2,1,0:T(8,128)(2,1)S(1)}, bf16[1,64,4096]{2,1,0:T(8,128)(2,1)S(1)}, u32[]{:S(2)}, u32[]{:S(2)}) collective-permute-start(bf16[1,64,4096]{2,1,0:T(8,128)(2,1)S(1)} %get-tuple-element.151), channel_id=1, source_target_pairs={{0,8},{8,0},{4,12},{12,4},{16,24},{24,16},{20,28},{28,20},{1,9},{9... | collective-permute-start | bytes 1572872 | tf_op jit(solution)/shard_map/ppermute | solution.py:14
  12.9 13.9 %collective-permute-start.3 = (bf16[1,64,4096]{2,1,0:T(8,128)(2,1)S(1)}, bf16[1,64,4096]{2,1,0:T(8,128)(2,1)S(1)}, u32[]{:S(2)}, u32[]{:S(2)}) collective-permute-start(bf16[1,64,4096]{2,1,0:T(8,128)(2,1)S(1)} %get-tuple-element.152), channel_id=1, source_target_pairs={{0,16},{16,0},{4,20},{20,4},{8,24},{24,8},{12,28},{28,12},{1,17},{... | collective-permute-start | bytes 1572872 | tf_op jit(solution)/shard_map/ppermute | solution.py:14
  24.9 24.4 %collective-permute-start.1 = (bf16[2,64,4096]{2,1,0:T(8,128)(2,1)S(1)}, bf16[2,64,4096]{2,1,0:T(8,128)(2,1)S(1)}, u32[]{:S(2)}, u32[]{:S(2)}) collective-permute-start(bf16[2,64,4096]{2,1,0:T(8,128)(2,1)S(1)} %pad_maximum_fusion.8), channel_id=1, source_target_pairs={{0,16},{16,0},{4,20},{20,4},{8,24},{24,8},{12,28},{28,12},{1,17},{... | collective-permute-start | bytes 3145736 | tf_op jit(solution)/shard_map/ppermute | solution.py:14
  27.8 32.5 %collective-permute-start.4 = (bf16[2,64,4096]{2,1,0:T(8,128)(2,1)}, bf16[2,64,4096]{2,1,0:T(8,128)(2,1)}, u32[]{:S(2)}, u32[]{:S(2)}) collective-permute-start(bf16[2,64,4096]{2,1,0:T(8,128)(2,1)} %pad_maximum_fusion.9), channel_id=1, source_target_pairs={{0,8},{8,0},{4,12},{12,4},{16,24},{24,16},{20,28},{28,20},{1,9},{9... | collective-permute-start | bytes 3145736 | tf_op jit(solution)/shard_map/ppermute | solution.py:14
  51.9 66.3 %collective-permute-start.2 = (bf16[4,64,4096]{2,1,0:T(8,128)(2,1)}, bf16[4,64,4096]{2,1,0:T(8,128)(2,1)}, u32[]{:S(2)}, u32[]{:S(2)}) collective-permute-start(bf16[4,64,4096]{2,1,0:T(8,128)(2,1)} %pad_maximum_fusion.3), channel_id=1, source_target_pairs={{0,4},{4,0},{8,12},{12,8},{16,20},{20,16},{24,28},{28,24},{1,5},{5... | collective-permute-start | bytes 6291464 | tf_op jit(solution)/shard_map/ppermute | solution.py:14
  55.5 57.2 %all-to-all-start.2 = ((bf16[4,128,1024]{2,1,0:T(8,128)(2,1)}), bf16[4,128,1024]{2,1,0:T(8,128)(2,1)S(1)}, u32[]{:S(2)}, u32[]{:S(2)}) async-start(bf16[4,128,1024]{2,1,0:T(8,128)(2,1)} %bitcast.233), calls=%async_computation.2 | async-start | bytes 2097152 | tf_op jit(solution)/shard_map/all_to_all | solution.py:108
  63.1 72.1 %collective-permute-start.5 = (bf16[4,64,4096]{2,1,0:T(8,128)(2,1)}, bf16[4,64,4096]{2,1,0:T(8,128)(2,1)}, u32[]{:S(2)}, u32[]{:S(2)}) collective-permute-start(bf16[4,64,4096]{2,1,0:T(8,128)(2,1)} %pad_maximum_fusion.4), channel_id=1, source_target_pairs={{0,4},{4,0},{8,12},{12,8},{16,20},{20,16},{24,28},{28,24},{1,5},{5... | collective-permute-start | bytes 6291464 | tf_op jit(solution)/shard_map/ppermute | solution.py:14
  113.7 54.4 %all-to-all-start = ((bf16[128,8,512]{0,2,1:T(8,128)(2,1)}), bf16[128,8,512]{0,2,1:T(8,128)(2,1)S(1)}, u32[]{:S(2)}, u32[]{:S(2)}) async-start(bf16[128,8,512]{0,2,1:T(8,128)(2,1)} %bitcast.232), calls=%async_computation | async-start | bytes 2097152 | tf_op jit(solution)/shard_map/all_to_all | solution.py:138
  117.4 153.9 %all-gather.7.cloned.1.call-start = ((), (), s32[]{:S(2)}) async-start(), calls=%async_computation.4 | async-start | bytes 9437184 | tf_op jit(solution)/shard_map/all_gather | solution.py:153
  118.1 228.2 %all-gather.9.cloned.1.call-start = ((), (), s32[]{:S(2)}) async-start(), calls=%async_computation.5 | async-start | bytes 6553600 | tf_op jit(solution)/shard_map/all_gather | solution.py:150
  135.3 16.9 %collective-permute-start.6 = (bf16[4096,128]{1,0:T(8,128)(2,1)}, bf16[4096,128]{1,0:T(8,128)(2,1)}, u32[]{:S(2)}, u32[]{:S(2)}) collective-permute-start(bf16[4096,128]{1,0:T(8,128)(2,1)} %slice.50), channel_id=1, source_target_pairs={{0,4},{4,0},{8,12},{12,8},{16,20},{20,16},{24,28},{28,24},{1,5},{5... | collective-permute-start | bytes 3145736 | tf_op jit(solution)/shard_map/ppermute | solution.py:14
  152.2 5.8 %slice-start = ((bf16[4096,640]{1,0:T(8,128)(2,1)}), bf16[4096,512]{1,0:T(8,128)(2,1)S(1)}, s32[]{:S(2)}) async-start(bf16[4096,640]{1,0:T(8,128)(2,1)} %all-gather.5.cloned.1.call-done), calls=%async_computation.6 | async-start | bytes 8388608 | tf_op jit(solution)/shard_map/slice | solution.py:119
  168.1 62.8 %copy-start.19 = (s32[8,8]{0,1:T(8,128)S(1)}, s32[8,8]{0,1:T(8,128)}, u32[]{:S(2)}) copy-start(s32[8,8]{0,1:T(8,128)} %copy.74) | copy-start | bytes 772
  168.1 62.8 %copy-start.20 = (pred[8,8]{0,1:T(8,128)(4,1)S(1)}, pred[8,8]{0,1:T(8,128)(4,1)}, u32[]{:S(2)}) copy-start(pred[8,8]{0,1:T(8,128)(4,1)} %iota_compare_fusion.1) | copy-start | bytes 196
  168.3 5.3 %copy-start.4 = (bf16[2,4,128,4,128]{2,4,3,1,0:T(8,128)(2,1)}, bf16[2,4,128,4,128]{2,4,3,1,0:T(8,128)(2,1)S(1)}, u32[]{:S(2)}) copy-start(bf16[2,4,128,4,128]{2,4,3,1,0:T(8,128)(2,1)S(1)} %get-tuple-element.264) | copy-start | bytes 3145732 | tf_op jit(solution)/shard_map/while
  171.8 5.2 %copy-start.9 = (f32[2,4,8,128,128]{4,3,2,1,0:T(8,128)S(1)}, f32[2,4,8,128,128]{4,3,2,1,0:T(8,128)}, u32[]{:S(2)}) copy-start(f32[2,4,8,128,128]{4,3,2,1,0:T(8,128)} %get-tuple-element.246) | copy-start | bytes 12582916 | tf_op jit(solution)/shard_map/while
  182.1 7.8 %copy-start.3 = (f32[4,8,128,128,4]{3,2,4,1,0:T(8,128)S(1)}, f32[4,8,128,128,4]{3,2,4,1,0:T(8,128)}, u32[]{:S(2)}) copy-start(f32[4,8,128,128,4]{3,2,4,1,0:T(8,128)} %copy-done.2) | copy-start | bytes 25165828 | tf_op jit(solution)/shard_map/while
  213.3 7.8 %copy-start.3 = (f32[4,8,128,128,4]{3,2,4,1,0:T(8,128)S(1)}, f32[4,8,128,128,4]{3,2,4,1,0:T(8,128)}, u32[]{:S(2)}) copy-start(f32[4,8,128,128,4]{3,2,4,1,0:T(8,128)} %copy-done.2) | copy-start | bytes 25165828 | tf_op jit(solution)/shard_map/while
  230.9 7.4 %copy-start.11 = (f32[2,4,8,128,128]{4,3,2,1,0:T(8,128)S(1)}, f32[2,4,8,128,128]{4,3,2,1,0:T(8,128)}, u32[]{:S(2)}) copy-start(f32[2,4,8,128,128]{4,3,2,1,0:T(8,128)} %get-tuple-element.66) | copy-start | bytes 12582916
  238.2 6.6 %copy-start.18 = (bf16[2,4,128,4,128]{4,3,2,1,0:T(4,128)(2,1)S(1)}, bf16[2,4,128,4,128]{4,3,2,1,0:T(4,128)(2,1)}, u32[]{:S(2)}) copy-start(bf16[2,4,128,4,128]{4,3,2,1,0:T(4,128)(2,1)} %get-tuple-element.64) | copy-start | bytes 3145732
  244.4 5.4 %copy-start.17 = (bf16[2,4,128,4,128]{2,4,3,1,0:T(8,128)(2,1)S(1)}, bf16[2,4,128,4,128]{2,4,3,1,0:T(8,128)(2,1)}, u32[]{:S(2)}) copy-start(bf16[2,4,128,4,128]{2,4,3,1,0:T(8,128)(2,1)} %get-tuple-element.63) | copy-start | bytes 3145732
  244.4 3.1 collective-permute-start.7
  (20 other events, 58.1 us)
Sparse Core Ops, SparseCore 0:
  9.9 123.0 all-gather.4
  134.9 52.6 all-gather.6
  249.9 96.3 all-gather.8
